TPU v7x, 256 devices: a whole 4x4x8 slice. The times are simulated.
256 devices in a mesh: dp: 8 (over y, core), expert: 32 (over z, x).
Axes of the slice: x: 4, y: 4, z: 8, core: 2. Of those that a mesh axis runs over, the one named last changes fastest.
Arguments:
- tokens: bfloat16 [4096, 4096], P('expert', 'dp'), may hold values from -6 to 6
- expert_ids: int32 [4096, 8], P('expert'), may hold values from 0 to 63, all different within a row; in each aligned block of 128 rows (0 to 127, 128 to 255, ...) at most 24 rows name the same one
- route_weights: float32 [4096, 8], P('expert'), may hold values from 0.1 to 0.4
- gate_up_weight: bfloat16 [64, 4096, 1536], P('expert', 'dp'), may hold values from -0.09375 to 0.09375
- down_weight: bfloat16 [64, 768, 4096], P('expert', None, 'dp'), may hold values from -0.21875 to 0.21875
- out_grad: bfloat16 [4096, 4096], P('expert', 'dp'), may hold values from -6 to 6
Outputs:
- layer_out: bfloat16 [4096, 4096], P('expert', 'dp')
- token_grad: bfloat16 [4096, 4096], P('expert', 'dp')
- route_grad: float32 [4096, 8], P('expert')
- gate_up_grad: bfloat16 [64, 4096, 1536], P('expert', 'dp')
- down_grad: bfloat16 [64, 768, 4096], P('expert', None, 'dp')
Inputs may be any that keep to these rules, and one draw needn't show every extreme that they name: `expert_ids`: each row names 8 different experts. Among the 128 rows of one group no expert is named more than 24 times, and in every draw some group names some expert exactly 24 times.
All inputs are finite; a program needn't handle non-finite values.
Results may differ from a plain program's by a relative error of at most 0.029.
Values may be sent and summed in bfloat16 or wider, within the bound.
No kernel may reach another device: no remote copies, remote signals or barrier semaphores. Data moves between devices by JAX's collectives and lax.ppermute only.
A program may use at most 128 MiB of HBM per device.

v0:
```python
import jax
import jax.numpy as jnp
from jax import lax
from jax.sharding import PartitionSpec as P


def layer(tokens, expert_ids, route_weights, gate_up_weight, down_weight, out_grad):
    tok_count, piece_width = tokens.shape
    top_count = expert_ids.shape[1]
    group_count = lax.axis_size("expert")
    local_count = gate_up_weight.shape[0]
    hidden_units = down_weight.shape[1]
    expert_total = local_count * group_count
    capacity = 3 * tok_count * top_count // (2 * expert_total)
    slot_count = expert_total * capacity
    rows_all = group_count * capacity
    route_count = tok_count * top_count
    block_shape = (local_count, group_count, capacity, piece_width)
    route_ids = expert_ids.reshape(-1)
    onehot = (route_ids[:, None] == jnp.arange(expert_total, dtype=jnp.int32)[None, :]).astype(
        jnp.bfloat16
    )
    order = jnp.arange(route_count, dtype=jnp.int32)
    lower = (order[None, :] < order[:, None]).astype(jnp.bfloat16)
    earlier = jnp.dot(lower, onehot, preferred_element_type=jnp.float32)
    slot_rank = jnp.sum(onehot.astype(jnp.float32) * earlier, axis=1).astype(jnp.int32)
    slot_index = (
        route_ids % local_count * rows_all + route_ids // local_count * capacity + slot_rank
    )
    route_hit = slot_index[:, None] == jnp.arange(slot_count, dtype=jnp.int32)[None, :]
    token_hit = jnp.any(route_hit.reshape(tok_count, top_count, slot_count), axis=1).astype(
        jnp.bfloat16
    )
    weight_flat = route_weights.reshape(-1)
    slot_weight = jnp.sum(jnp.where(route_hit, weight_flat[:, None], 0.0), axis=0)
    outbound = lax.dot_general(
        token_hit, tokens, (((0,), (0,)), ((), ())), preferred_element_type=jnp.float32
    ).astype(jnp.bfloat16)
    grad_outbound = (
        slot_weight[:, None]
        * lax.dot_general(
            token_hit, out_grad, (((0,), (0,)), ((), ())), preferred_element_type=jnp.float32
        )
    ).astype(jnp.bfloat16)
    arrived = lax.all_to_all(
        outbound.reshape(block_shape), "expert", split_axis=1, concat_axis=1, tiled=True
    ).reshape(local_count, rows_all, piece_width)
    preact = lax.psum(
        jnp.einsum(
            "lrk,lkf->rlf", arrived, gate_up_weight, preferred_element_type=jnp.float32
        ).astype(jnp.bfloat16),
        "dp",
    ).astype(jnp.float32)
    grad_arrived = lax.all_to_all(
        grad_outbound.reshape(block_shape), "expert", split_axis=1, concat_axis=1, tiled=True
    ).reshape(local_count, rows_all, piece_width)
    preact, grad_arrived = lax.optimization_barrier((preact, grad_arrived))
    gate_pre = preact[..., :hidden_units]
    up_pre = preact[..., hidden_units:]
    sigmoid_gate = jax.nn.sigmoid(gate_pre)
    activation = gate_pre * sigmoid_gate
    hidden_all = (activation * up_pre).astype(jnp.bfloat16)
    out_slice = jnp.einsum(
        "rlf,lfk->lrk", hidden_all, down_weight, preferred_element_type=jnp.float32
    ).astype(jnp.bfloat16)
    out_slice, grad_arrived = lax.optimization_barrier((out_slice, grad_arrived))
    hidden_grad_part = jnp.einsum(
        "lrk,lfk->rlf", grad_arrived, down_weight, preferred_element_type=jnp.float32
    ).astype(jnp.bfloat16)
    hidden_grad = lax.psum(hidden_grad_part, "dp")
    hidden_grad = hidden_grad.astype(jnp.float32)
    gate_grad = hidden_grad * up_pre * sigmoid_gate * (1.0 + gate_pre * (1.0 - sigmoid_gate))
    up_grad = hidden_grad * activation
    preact_grad_all = jnp.concatenate([gate_grad, up_grad], axis=2).astype(jnp.bfloat16)
    grad_routes = jnp.repeat(out_grad, top_count, axis=0).astype(jnp.float32)
    returned = lax.all_to_all(
        out_slice.reshape(block_shape), "expert", split_axis=1, concat_axis=1, tiled=True
    )
    route_pick = route_hit.astype(jnp.bfloat16)
    y_routes = jnp.dot(
        route_pick, returned.reshape(slot_count, piece_width), preferred_element_type=jnp.float32
    )
    layer_out = (
        (weight_flat[:, None] * y_routes)
        .reshape(tok_count, top_count, piece_width)
        .sum(axis=1)
        .astype(jnp.bfloat16)
    )
    partial_dot = jnp.sum(grad_routes * y_routes, axis=1).reshape(tok_count, top_count)
    route_grad = lax.psum(partial_dot, "dp")
    x_grad_slice = jnp.einsum(
        "rlf,lkf->lrk", preact_grad_all, gate_up_weight, preferred_element_type=jnp.float32
    ).astype(jnp.bfloat16)
    gate_up_grad = jnp.einsum(
        "lrk,rlf->lkf", arrived, preact_grad_all, preferred_element_type=jnp.float32
    ).astype(jnp.bfloat16)
    down_grad = jnp.einsum(
        "rlf,lrk->lfk", hidden_all, grad_arrived, preferred_element_type=jnp.float32
    ).astype(jnp.bfloat16)
    grad_back = lax.all_to_all(
        x_grad_slice.reshape(block_shape), "expert", split_axis=1, concat_axis=1, tiled=True
    )
    token_grad = jnp.dot(
        token_hit, grad_back.reshape(slot_count, piece_width), preferred_element_type=jnp.float32
    ).astype(jnp.bfloat16)
    return (layer_out, token_grad, route_grad, gate_up_grad, down_grad)


def solution(mesh):
    placed = (
        P("expert", "dp"),
        P("expert", None),
        P("expert", None),
        P("expert", "dp", None),
        P("expert", None, "dp"),
        P("expert", "dp"),
    )
    return jax.shard_map(
        layer,
        mesh=mesh,
        in_specs=placed,
        out_specs=(
            P("expert", "dp"),
            P("expert", "dp"),
            P("expert", None),
            P("expert", "dp", None),
            P("expert", None, "dp"),
        ),
        check_vma=False,
    )
```

profile of v0, /device:TPU:2, one launch (start us, length us, event | category | flops | bytes accessed | tf_op | source)
XLA Modules:
  0.0 326.3 jit_solution(3122651912128517981)
XLA Ops:
  7.2 0.0 copy-start
  7.2 0.0 copy-start.10
  7.2 1.0 copy.55
  8.1 0.1 reshape.114
  8.2 0.6 fusion.14
  8.9 0.1 convert_element_type.76
  8.9 0.1 fusion.19
  9.0 3.2 fusion.1
  12.2 0.0 copy-done.10
  12.2 0.6 convolution_convert_fusion.1
  12.8 0.0 copy-start.11
  12.8 1.3 copy.60
  14.2 11.8 %all-to-all-start = ((bf16[2,32,24,512]{3,2,0,1:T(8,128)(2,1)}), bf16[2,32,24,512]{3,2,0,1:T(8,128)(2,1)}, u32[]{:S(2)}, u32[]{:S(2)}) async-start(bf16[2,32,24,512]{3,2,0,1:T(8,128)(2,1)} %copy.60), calls=%async_computation | async-start | bytes 3145728 | tf_op jit(solution)/shard_map/all_to_all | solution.py:45
  26.0 0.0 copy-done.11
  26.0 0.1 copy.54
  26.1 0.1 mul.75
  26.2 0.8 select_reduce_fusion
  27.0 0.0 copy-done.9
  27.0 0.6 fusion.10
  27.7 1.3 copy.62
  29.0 35.4 %all-to-all-done = bf16[2,32,24,512]{3,2,0,1:T(8,128)(2,1)} async-done(((bf16[2,32,24,512]{3,2,0,1:T(8,128)(2,1)}), bf16[2,32,24,512]{3,2,0,1:T(8,128)(2,1)}, u32[]{:S(2)}, u32[]{:S(2)}) %all-to-all-start) | async-done | bytes 1572896 | tf_op jit(solution)/shard_map/all_to_all | solution.py:45
  64.4 6.6 %all-to-all-start.1 = ((bf16[2,32,24,512]{3,2,0,1:T(8,128)(2,1)}), bf16[2,32,24,512]{3,2,0,1:T(8,128)(2,1)}, u32[]{:S(2)}, u32[]{:S(2)}) async-start(bf16[2,32,24,512]{3,2,0,1:T(8,128)(2,1)} %copy.62), calls=%async_computation.1 | async-start | bytes 3145728 | tf_op jit(solution)/shard_map/all_to_all | solution.py:54
  70.9 0.0 all-reduce.3.cloned.1.call-start
  71.0 1.5 copy.61
  72.5 1.2 copy-done.7
  73.7 4.2 %convert_bitcast_fusion = bf16[768,2,1536]{2,0,1:T(8,128)(2,1)} fusion(bf16[2,768,512]{2,1,0:T(8,128)(2,1)S(1)} %bitcast.38, bf16[2,512,1536]{2,1,0:T(8,128)(2,1)S(1)} %copy-done), kind=kOutput, calls=%fused_computation.15 | convolution fusion | flops 2418278400 | bytes 9437184 | tf_op jit(solution)/shard_map/lrk,lkf->rlf/dot_general | solution.py:49
  77.9 0.0 all-reduce.3.cloned.1.call-update
  77.9 30.7 %all-to-all-done.1 = bf16[2,32,24,512]{3,2,0,1:T(8,128)(2,1)} async-done(((bf16[2,32,24,512]{3,2,0,1:T(8,128)(2,1)}), bf16[2,32,24,512]{3,2,0,1:T(8,128)(2,1)}, u32[]{:S(2)}, u32[]{:S(2)}) %all-to-all-start.1) | async-done | bytes 1572896 | tf_op jit(solution)/shard_map/all_to_all | solution.py:54
  108.6 2.7 copy.63
  111.3 47.9 %all-reduce.3.cloned.1.call-done = bf16[768,2,1536]{2,0,1:T(8,128)(2,1)} async-done(((bf16[768,2,1536]{2,0,1:T(8,128)(2,1)}), bf16[768,2,1536]{2,0,1:T(8,128)(2,1)}) %all-reduce.3.cloned.1.call-update) | async-done | bytes 4718608 | tf_op jit(solution)/shard_map/psum | solution.py:48
  159.2 3.6 %convert_element_type.80 = f32[768,2,1536]{2,0,1:T(8,128)S(1)} convert(bf16[768,2,1536]{2,0,1:T(8,128)(2,1)} %all-reduce.3.cloned.1.call-done) | non-fusion elementwise | flops 2359296 | bytes 14155776 | tf_op jit(solution)/shard_map/convert_element_type | solution.py:53
  162.8 0.0 copy-start.12
  162.8 1.6 multiply_convert_fusion
  164.4 2.1 copy-done.1
  166.5 1.4 convolution_convert_fusion.3
  167.9 0.0 copy-done.2
  167.9 1.4 copy.64
  169.3 10.2 %all-to-all-start.2 = ((bf16[2,32,24,512]{3,2,0,1:T(8,128)(2,1)}), bf16[2,32,24,512]{3,2,0,1:T(8,128)(2,1)}, u32[]{:S(2)}, u32[]{:S(2)}) async-start(bf16[2,32,24,512]{3,2,0,1:T(8,128)(2,1)} %copy.64), calls=%async_computation.2 | async-start | bytes 3145728 | tf_op jit(solution)/shard_map/all_to_all | solution.py:76
  179.5 0.2 all-reduce.5.cloned.1.call-start
  179.7 4.7 %convert_bitcast_fusion.1 = bf16[768,2,768]{2,0,1:T(8,128)(2,1)} fusion(bf16[2,768,512]{2,1,0:T(8,128)(2,1)} %bitcast.40, bf16[2,768,512]{2,1,0:T(8,128)(2,1)} %param.10), kind=kOutput, calls=%fused_computation.24 | convolution fusion | flops 1209139200 | bytes 5505024 | tf_op jit(solution)/shard_map/lrk,lfk->rlf/dot_general | solution.py:67
  184.4 0.0 all-reduce.5.cloned.1.call-update
  184.4 71.9 %all-reduce.5.cloned.1.call-done = bf16[768,2,768]{2,0,1:T(8,128)(2,1)} async-done(((bf16[768,2,768]{2,0,1:T(8,128)(2,1)}), bf16[768,2,768]{2,0,1:T(8,128)(2,1)}) %all-reduce.5.cloned.1.call-update) | async-done | bytes 2359312 | tf_op jit(solution)/shard_map/psum | solution.py:70
  256.4 5.7 %fusion.4 = (bf16[768,2,768]{2,0,1:T(8,128)(2,1)S(1)}, bf16[768,2,768]{2,0,1:T(8,128)(2,1)S(1)}) fusion(bf16[768,2,768]{2,0,1:T(8,128)(2,1)} %all-reduce.5.cloned.1.call-done, f32[768,2,1536]{2,0,1:T(8,128)} %copy-done.1), kind=kLoop, calls=%fused_computation.9 | loop fusion | flops 16515072 | bytes 16515072 | tf_op jit(solution)/shard_map/convert
  262.1 0.0 copy-start.5
  262.1 2.6 fusion.12
  264.7 0.0 copy-done.3
  264.7 0.0 copy-done.5
  264.8 1.3 copy.66
  266.1 0.0 all-to-all-done.2
  266.1 10.2 %all-to-all-start.3 = ((bf16[2,32,24,512]{3,2,0,1:T(8,128)(2,1)}), bf16[2,32,24,512]{3,2,0,1:T(8,128)(2,1)}, u32[]{:S(2)}, u32[]{:S(2)}) async-start(bf16[2,32,24,512]{3,2,0,1:T(8,128)(2,1)} %copy.66), calls=%async_computation.3 | async-start | bytes 3145728 | tf_op jit(solution)/shard_map/all_to_all | solution.py:100
  276.3 0.0 copy-start.4
  276.3 0.0 copy-start.6
  276.3 4.8 %convolution_convert_fusion.2 = bf16[2,768,512]{2,1,0:T(8,128)(2,1)} fusion(bf16[768,2,768]{2,0,1:T(8,128)(2,1)} %copy-done.2, bf16[2,768,512]{2,1,0:T(8,128)(2,1)} %bitcast.41), kind=kOutput, calls=%fused_computation.29 | convolution fusion | flops 1208745984 | bytes 5505024 | tf_op jit(solution)/shard_map/rlf,lrk->lfk/dot_general | solution.py:97
  281.2 0.0 copy-done.6
  281.2 4.1 %convolution_convert_fusion = bf16[2,512,1536]{2,1,0:T(8,128)(2,1)} fusion(bf16[2,768,512]{2,1,0:T(8,128)(2,1)S(1)} %bitcast.39, bf16[768,2,768]{2,0,1:T(8,128)(2,1)S(1)} %copy-done.6, bf16[768,2,768]{2,0,1:T(8,128)(2,1)S(1)} %copy-done.4), kind=kOutput, calls=%fused_computation.18 | convolution fusion | flops 2426929152 | bytes 9437184 | tf_op jit(solution)/shard_map/lrk,rlf->lkf/dot_general | solution.py:94
  285.3 1.5 copy.65
  286.8 2.9 bitcast_reduce_fusion
  289.7 0.3 fusion.11
  290.0 0.1 reshape.124
  290.0 26.2 %psum.23 = f32[128,8]{1,0:T(8,128)S(1)} all-reduce(f32[128,8]{1,0:T(8,128)S(1)} %reshape.124), channel_id=1, replica_groups=mesh['dp'=8,'expert'=32] {'dp'}, use_global_device_ids=true, to_apply=%region_7.8 | all-reduce | flops 1024 | bytes 8192 | tf_op jit(solution)/shard_map/psum | solution.py:90
  316.2 0.7 copy.70
  316.9 0.0 all-to-all-done.3
  316.9 1.5 copy.67
  318.4 1.0 convolution_convert_fusion.4
  (13 shorter events, 0.1 us)
Async XLA Ops:
  7.2 66.5 %copy-start = (bf16[2,512,1536]{2,1,0:T(8,128)(2,1)S(1)}, bf16[2,512,1536]{2,1,0:T(8,128)(2,1)}, u32[]{:S(2)}) copy-start(bf16[2,512,1536]{2,1,0:T(8,128)(2,1)} %param.9) | copy-start | bytes 9437188
  7.2 5.0 %copy-start.10 = (bf16[128,512]{1,0:T(8,128)(2,1)S(1)}, bf16[128,512]{1,0:T(8,128)(2,1)}, u32[]{:S(2)}) copy-start(bf16[128,512]{1,0:T(8,128)(2,1)} %param.6) | copy-start | bytes 393220
  12.8 13.2 %copy-start.11 = (f32[128,8]{0,1:T(8,128)S(1)}, f32[128,8]{0,1:T(8,128)}, u32[]{:S(2)}) copy-start(f32[128,8]{0,1:T(8,128)} %param.8) | copy-start | bytes 12292
  14.2 12.9 %copy-start.9 = (bf16[128,512]{1,0:T(8,128)(2,1)S(1)}, bf16[128,512]{1,0:T(8,128)(2,1)}, u32[]{:S(2)}) copy-start(bf16[128,512]{1,0:T(8,128)(2,1)} %param.11) | copy-start | bytes 393220
  14.2 50.2 %all-to-all-start = ((bf16[2,32,24,512]{3,2,0,1:T(8,128)(2,1)}), bf16[2,32,24,512]{3,2,0,1:T(8,128)(2,1)}, u32[]{:S(2)}, u32[]{:S(2)}) async-start(bf16[2,32,24,512]{3,2,0,1:T(8,128)(2,1)} %copy.60), calls=%async_computation | async-start | bytes 3145728 | tf_op jit(solution)/shard_map/all_to_all | solution.py:45
  64.4 44.3 %all-to-all-start.1 = ((bf16[2,32,24,512]{3,2,0,1:T(8,128)(2,1)}), bf16[2,32,24,512]{3,2,0,1:T(8,128)(2,1)}, u32[]{:S(2)}, u32[]{:S(2)}) async-start(bf16[2,32,24,512]{3,2,0,1:T(8,128)(2,1)} %copy.62), calls=%async_computation.1 | async-start | bytes 3145728 | tf_op jit(solution)/shard_map/all_to_all | solution.py:54
  70.9 88.2 %all-reduce.3.cloned.1.call-start = ((), (), s32[]{:S(2)}) async-start(), calls=%async_computation.4 | async-start | bytes 9437184 | tf_op jit(solution)/shard_map/psum | solution.py:48
  72.5 1.2 copy-start.7
  162.8 3.7 %copy-start.1 = (f32[768,2,1536]{2,0,1:T(8,128)}, f32[768,2,1536]{2,0,1:T(8,128)S(1)}, u32[]{:S(2)}) copy-start(f32[768,2,1536]{2,0,1:T(8,128)S(1)} %convert_element_type.80) | copy-start | bytes 28311556
  162.8 3.7 %copy-start.12 = (bf16[2,768,512]{2,1,0:T(8,128)(2,1)S(1)}, bf16[2,768,512]{2,1,0:T(8,128)(2,1)}, u32[]{:S(2)}) copy-start(bf16[2,768,512]{2,1,0:T(8,128)(2,1)} %param.10) | copy-start | bytes 4718596
  166.5 1.4 copy-start.2
  169.3 96.8 %all-to-all-start.2 = ((bf16[2,32,24,512]{3,2,0,1:T(8,128)(2,1)}), bf16[2,32,24,512]{3,2,0,1:T(8,128)(2,1)}, u32[]{:S(2)}, u32[]{:S(2)}) async-start(bf16[2,32,24,512]{3,2,0,1:T(8,128)(2,1)} %copy.64), calls=%async_computation.2 | async-start | bytes 3145728 | tf_op jit(solution)/shard_map/all_to_all | solution.py:76
  179.5 76.9 %all-reduce.5.cloned.1.call-start = ((), (), s32[]{:S(2)}) async-start(), calls=%async_computation.5 | async-start | bytes 4718592 | tf_op jit(solution)/shard_map/psum | solution.py:70
  262.1 2.7 copy-start.3
  262.1 2.7 copy-start.5
  266.1 50.8 %all-to-all-start.3 = ((bf16[2,32,24,512]{3,2,0,1:T(8,128)(2,1)}), bf16[2,32,24,512]{3,2,0,1:T(8,128)(2,1)}, u32[]{:S(2)}, u32[]{:S(2)}) async-start(bf16[2,32,24,512]{3,2,0,1:T(8,128)(2,1)} %copy.66), calls=%async_computation.3 | async-start | bytes 3145728 | tf_op jit(solution)/shard_map/all_to_all | solution.py:100
  276.3 4.9 %copy-start.4 = (bf16[768,2,768]{2,0,1:T(8,128)(2,1)S(1)}, bf16[768,2,768]{2,0,1:T(8,128)(2,1)}, u32[]{:S(2)}) copy-start(bf16[768,2,768]{2,0,1:T(8,128)(2,1)} %copy-done.3) | copy-start | bytes 7077892
  276.3 4.9 %copy-start.6 = (bf16[768,2,768]{2,0,1:T(8,128)(2,1)S(1)}, bf16[768,2,768]{2,0,1:T(8,128)(2,1)}, u32[]{:S(2)}) copy-start(bf16[768,2,768]{2,0,1:T(8,128)(2,1)} %copy-done.5) | copy-start | bytes 7077892
  276.3 4.9 %copy-start.8 = (bf16[2,32,24,512]{3,2,1,0:T(8,128)(2,1)S(1)}, bf16[2,32,24,512]{3,2,1,0:T(8,128)(2,1)}, u32[]{:S(2)}) copy-start(bf16[2,32,24,512]{3,2,1,0:T(8,128)(2,1)} %copy-done.7) | copy-start | bytes 4718596
Sparse Core Ops, SparseCore 0:
  78.1 81.0 all-reduce.2
  184.6 71.7 all-reduce.4
where the time goes:
time: 327 us; the launch traced here: 326 us
  waiting for transfers between devices  186 us (57%)
  starting transfers between devices  39 us (12%)
  matrix products  27.7 us (8%)
  blocking collectives  26.2 us (8%)
  local copies, waits for them, and re-layouts  17.9 us (5%)
  other arithmetic  15.2 us (5%)
  between operations  14.4 us (4%)
    psum x1, waiting for transfers between devices, layer(): hidden_grad = lax.psum(hidden_grad_part, 'dp')  71.9 us
    psum x1, waiting for transfers between devices, layer(): lax.psum(jnp.einsum('lrk,lkf->rlf', arrived, gate_up_weight, preferred_el...  47.9 us
    all_to_all x1, waiting for transfers between devices, layer(): lax.all_to_all(outbound.reshape(block_shape), 'expert', split_axis=1, con...  35.4 us
    all_to_all x1, waiting for transfers between devices, layer(): lax.all_to_all(grad_outbound.reshape(block_shape), 'expert', split_axis=1...  30.7 us
    psum x1, blocking collectives, layer(): route_grad = lax.psum(partial_dot, 'dp')  26.2 us
    all_to_all x1, starting transfers between devices, layer(): lax.all_to_all(outbound.reshape(block_shape), 'expert', split_axis=1, con...  11.8 us
    all_to_all x1, starting transfers between devices, layer(): lax.all_to_all(out_slice.reshape(block_shape), 'expert', split_axis=1, co...  10.2 us
    all_to_all x1, starting transfers between devices, layer(): lax.all_to_all(x_grad_slice.reshape(block_shape), 'expert', split_axis=1,...  10.2 us
  transfers between devices with their start and end apart: 6, of which 4 were waited for; matrix products, arithmetic and copies ran while one was open for 12% of the time, Pallas kernels for 0%

commit v1 on v0

--- a/solution.py
+++ b/solution.py
@@ -45,11 +45,13 @@
     arrived = lax.all_to_all(
         outbound.reshape(block_shape), "expert", split_axis=1, concat_axis=1, tiled=True
     ).reshape(local_count, rows_all, piece_width)
-    preact = lax.psum(
+    preact = lax.psum_scatter(
         jnp.einsum(
             "lrk,lkf->rlf", arrived, gate_up_weight, preferred_element_type=jnp.float32
         ).astype(jnp.bfloat16),
         "dp",
+        scatter_dimension=0,
+        tiled=True,
     ).astype(jnp.float32)
     grad_arrived = lax.all_to_all(
         grad_outbound.reshape(block_shape), "expert", split_axis=1, concat_axis=1, tiled=True
@@ -59,19 +61,22 @@
     up_pre = preact[..., hidden_units:]
     sigmoid_gate = jax.nn.sigmoid(gate_pre)
     activation = gate_pre * sigmoid_gate
-    hidden_all = (activation * up_pre).astype(jnp.bfloat16)
+    hidden_mine = (activation * up_pre).astype(jnp.bfloat16)
+    hidden_mine, grad_arrived = lax.optimization_barrier((hidden_mine, grad_arrived))
+    hidden_all = lax.all_gather(hidden_mine, "dp", axis=0, tiled=True)
+    hidden_grad_part = jnp.einsum(
+        "lrk,lfk->rlf", grad_arrived, down_weight, preferred_element_type=jnp.float32
+    ).astype(jnp.bfloat16)
+    hidden_grad = lax.psum_scatter(hidden_grad_part, "dp", scatter_dimension=0, tiled=True)
+    hidden_all, _ = lax.optimization_barrier((hidden_all, hidden_grad_part))
     out_slice = jnp.einsum(
         "rlf,lfk->lrk", hidden_all, down_weight, preferred_element_type=jnp.float32
     ).astype(jnp.bfloat16)
-    out_slice, grad_arrived = lax.optimization_barrier((out_slice, grad_arrived))
-    hidden_grad_part = jnp.einsum(
-        "lrk,lfk->rlf", grad_arrived, down_weight, preferred_element_type=jnp.float32
-    ).astype(jnp.bfloat16)
-    hidden_grad = lax.psum(hidden_grad_part, "dp")
     hidden_grad = hidden_grad.astype(jnp.float32)
     gate_grad = hidden_grad * up_pre * sigmoid_gate * (1.0 + gate_pre * (1.0 - sigmoid_gate))
     up_grad = hidden_grad * activation
-    preact_grad_all = jnp.concatenate([gate_grad, up_grad], axis=2).astype(jnp.bfloat16)
+    preact_grad = jnp.concatenate([gate_grad, up_grad], axis=2).astype(jnp.bfloat16)
+    preact_grad_all = lax.all_gather(preact_grad, "dp", axis=0, tiled=True)
     grad_routes = jnp.repeat(out_grad, top_count, axis=0).astype(jnp.float32)
     returned = lax.all_to_all(
         out_slice.reshape(block_shape), "expert", split_axis=1, concat_axis=1, tiled=True

time: 327 us -> 301 us (0.920)
  blocking collectives: 26.2 us -> 120 us
  waiting for transfers between devices: 186 us -> 92.7 us
  starting transfers between devices: 39 us -> 16.9 us
  matrix products: 27.7 us -> 34.9 us
  other arithmetic: 15.2 us -> 8.92 us
  local copies, waits for them, and re-layouts: 17.9 us -> 12.6 us
    psum x2 -> x0, waiting for transfers between devices: 120 us -> none  [the longest x1 71.9 us: layer(): hidden_grad = lax.psum(hidden_grad_part, 'dp')]
    all_to_all x0 -> x2, blocking collectives: none -> 94.6 us  [the longest x1 50.7 us: layer(): lax.all_to_all(outbound.reshape(block_shape), 'expert', split_axis=1, con...]
    all_to_all x2 -> x0, waiting for transfers between devices: 66.1 us -> none  [the longest x1 35.4 us: layer(): lax.all_to_all(outbound.reshape(block_shape), 'expert', split_axis=1, con...]
    all_gather x0 -> x2, waiting for transfers between devices: none -> 51 us  [the longest x1 26.4 us: layer(): hidden_all = lax.all_gather(hidden_mine, 'dp', axis=0, tiled=True)]
    reduce_scatter x0 -> x2, waiting for transfers between devices: none -> 33.2 us  [the longest x1 33.2 us: layer(): lax.psum_scatter(hidden_grad_part, 'dp', scatter_dimension=0, tiled=True)]
    all_to_all x2 -> x0, starting transfers between devices: 18.4 us -> none  [the longest x1 11.8 us: layer(): lax.all_to_all(outbound.reshape(block_shape), 'expert', split_axis=1, con...]
    all_to_all x1, waiting for transfers between devices: 0.01 us -> 7.74 us  [layer(): lax.all_to_all(out_slice.reshape(block_shape), 'expert', split_axis=1, co...]
    another operation x1, other arithmetic: 5.69 us -> 1.65 us
  transfers between devices with their start and end apart: 6 -> 6, of which waited for: 4 -> 4; matrix products, arithmetic and copies ran while one was open for 12% -> 11% of each run, Pallas kernels for 0% -> 0%
where the time goes in v1:
time: 301 us; the launch traced here: 300 us
  blocking collectives  120 us (40%)
  waiting for transfers between devices  92.7 us (31%)
  matrix products  34.9 us (12%)
  starting transfers between devices  16.9 us (6%)
  between operations  14 us (5%)
  local copies, waits for them, and re-layouts  12.6 us (4%)
  other arithmetic  8.92 us (3%)
    all_to_all x1, blocking collectives, layer(): lax.all_to_all(outbound.reshape(block_shape), 'expert', split_axis=1, con...  50.7 us
    all_to_all x1, blocking collectives, layer(): lax.all_to_all(grad_outbound.reshape(block_shape), 'expert', split_axis=1...  43.9 us
    reduce_scatter x1, waiting for transfers between devices, layer(): lax.psum_scatter(hidden_grad_part, 'dp', scatter_dimension=0, tiled=True)  33.2 us
    all_gather x1, waiting for transfers between devices, layer(): hidden_all = lax.all_gather(hidden_mine, 'dp', axis=0, tiled=True)  26.4 us
    psum x1, blocking collectives, layer(): route_grad = lax.psum(partial_dot, 'dp')  25.1 us
    all_gather x1, waiting for transfers between devices, layer(): preact_grad_all = lax.all_gather(preact_grad, 'dp', axis=0, tiled=True)  24.6 us
    all_to_all x1, starting transfers between devices, layer(): lax.all_to_all(out_slice.reshape(block_shape), 'expert', split_axis=1, co...  10.2 us
    all_to_all x1, waiting for transfers between devices, layer(): lax.all_to_all(out_slice.reshape(block_shape), 'expert', split_axis=1, co...  7.74 us
  transfers between devices with their start and end apart: 6, of which 4 were waited for; matrix products, arithmetic and copies ran while one was open for 11% of the time, Pallas kernels for 0%

profile of v1, /device:TPU:2, one launch (start us, length us, event | category | flops | bytes accessed | tf_op | source)
XLA Modules:
  0.0 299.8 jit_solution(15945599284697913905)
XLA Ops:
  7.2 0.0 copy-start
  7.2 0.0 copy-start.4
  7.2 0.0 reduce-scatter.3.cloned.1.call-start
  7.2 0.9 copy.55
  8.2 0.1 reshape.114
  8.3 0.6 fusion.7
  8.9 0.1 convert_element_type.76
  9.0 0.1 fusion.17
  9.1 3.2 %fusion.1 = pred[128,1536]{1,0:T(8,128)(4,1)S(1)} fusion(s32[128,8]{1,0:T(8,128)S(1)} %fusion.17), kind=kLoop, calls=%fused_computation.4 | loop fusion | flops 2949120 | bytes 200704 | tf_op jit(solution)/shard_map/reduce_or | solution.py:31
  12.2 0.0 copy-done.4
  12.2 0.6 convolution_convert_fusion.1
  12.8 0.2 copy.60
  13.1 50.7 %all_to_all.20 = bf16[2,32,24,512]{3,2,0,1:T(8,128)(2,1)S(1)} all-to-all(bf16[2,32,24,512]{3,2,0,1:T(8,128)(2,1)S(1)} %copy.60), channel_id=1, replica_groups=mesh['dp'=8,'expert'=32] {'expert'}, dimensions={1} | all-to-all | bytes 3145728 | tf_op jit(solution)/shard_map/all_to_all | solution.py:45
  63.8 0.1 copy.61
  63.9 0.0 copy-start.2
  63.9 1.2 copy-done.2
  65.1 0.0 copy-done
  65.1 4.2 %convert_bitcast_fusion = bf16[768,2,1536]{2,0,1:T(8,128)(2,1)} fusion(bf16[2,768,512]{2,1,0:T(8,128)(2,1)S(1)} %bitcast.40, bf16[2,512,1536]{2,1,0:T(8,128)(2,1)S(1)} %copy-done), kind=kOutput, calls=%fused_computation.5 | convolution fusion | flops 2418278400 | bytes 9437184 | tf_op jit(solution)/shard_map/lrk,lkf->rlf/dot_general | solution.py:49
  69.3 0.0 copy-start.5
  69.3 0.0 copy-start.3
  69.3 0.0 reduce-scatter.3.cloned.1.call-update
  69.3 0.0 reduce-scatter.5.cloned.1.call-start
  69.4 0.6 copy-done.5
  70.0 0.1 copy.54
  70.1 0.1 mul.75
  70.2 0.8 select_reduce_fusion
  71.0 0.0 copy-done.3
  71.0 0.6 fusion.4
  71.7 0.2 copy.62
  71.9 43.9 %all_to_all.21 = bf16[2,32,24,512]{3,2,0,1:T(8,128)(2,1)S(1)} all-to-all(bf16[2,32,24,512]{3,2,0,1:T(8,128)(2,1)S(1)} %copy.62), channel_id=1, replica_groups=mesh['dp'=8,'expert'=32] {'expert'}, dimensions={1} | all-to-all | bytes 3145728 | tf_op jit(solution)/shard_map/all_to_all | solution.py:56
  115.8 1.3 copy.63
  117.1 1.2 convert_element_type.80
  118.3 0.0 copy-start.1
  118.3 1.0 copy-done.1
  119.3 0.9 multiply_convert_fusion
  120.2 4.7 %convert_bitcast_fusion.1 = bf16[768,2,768]{2,0,1:T(8,128)(2,1)} fusion(bf16[2,768,512]{2,1,0:T(8,128)(2,1)} %bitcast.42, bf16[2,768,512]{2,1,0:T(8,128)(2,1)} %param.10), kind=kOutput, calls=%fused_computation.13 | convolution fusion | flops 1209139200 | bytes 5505024 | tf_op jit(solution)/shard_map/lrk,lfk->rlf/dot_general | solution.py:67
  124.9 0.0 reduce-scatter.5.cloned.1.call-update
  124.9 0.0 all-gather.3.cloned.1.call-start
  125.0 0.7 all-gather.3.cloned.1.call-update
  125.7 0.0 all-gather.5.cloned.1.call-start
  125.7 33.2 %reduce-scatter.5.cloned.1.call-done = bf16[96,2,768]{2,0,1:T(8,128)(2,1)} async-done(((bf16[768,2,768]{2,0,1:T(8,128)(2,1)}), bf16[96,2,768]{2,0,1:T(8,128)(2,1)}) %reduce-scatter.5.cloned.1.call-update) | async-done | bytes 294928 | tf_op jit(solution)/shard_map/reduce_scatter | solution.py:70
  158.9 1.6 fusion.10
  160.6 0.9 pad_maximum_fusion
  161.4 0.0 all-gather.5.cloned.1.call-update
  161.4 26.4 %all-gather.3.cloned.1.call-done = bf16[768,2,768]{2,0,1:T(8,128)(2,1)} async-done(((bf16[96,2,768]{2,0,1:T(8,128)(2,1)}), bf16[768,2,768]{2,0,1:T(8,128)(2,1)}) %all-gather.3.cloned.1.call-update) | async-done | bytes 2359312 | tf_op jit(solution)/shard_map/all_gather | solution.py:66
  187.8 3.5 %convolution_convert_fusion.3 = bf16[2,768,512]{2,1,0:T(8,128)(2,1)S(1)} fusion(bf16[768,2,768]{2,0,1:T(8,128)(2,1)} %all-gather.3.cloned.1.call-done, bf16[2,768,512]{2,1,0:T(8,128)(2,1)} %param.10), kind=kOutput, calls=%fused_computation.18 | convolution fusion | flops 1208745984 | bytes 5505024 | tf_op jit(solution)/shard_map/rlf,lfk->lrk/dot_general | solution.py:72
  191.3 1.4 copy.64
  192.7 10.2 %all-to-all-start.2 = ((bf16[2,32,24,512]{3,2,0,1:T(8,128)(2,1)}), bf16[2,32,24,512]{3,2,0,1:T(8,128)(2,1)}, u32[]{:S(2)}, u32[]{:S(2)}) async-start(bf16[2,32,24,512]{3,2,0,1:T(8,128)(2,1)} %copy.64), calls=%async_computation.3 | async-start | bytes 3145728 | tf_op jit(solution)/shard_map/all_to_all | solution.py:81
  202.9 24.6 %all-gather.5.cloned.1.call-done = bf16[768,2,1536]{2,0,1:T(8,128)(2,1)} async-done(((bf16[96,2,1536]{2,0,1:T(8,128)(2,1)}), bf16[768,2,1536]{2,0,1:T(8,128)(2,1)}) %all-gather.5.cloned.1.call-update) | async-done | bytes 4718608 | tf_op jit(solution)/shard_map/all_gather | solution.py:79
  227.5 5.0 %convolution_convert_fusion.4 = bf16[2,768,512]{2,1,0:T(8,128)(2,1)S(1)} fusion(bf16[768,2,1536]{2,0,1:T(8,128)(2,1)} %all-gather.5.cloned.1.call-done, bf16[2,512,1536]{2,1,0:T(8,128)(2,1)S(1)} %copy-done), kind=kOutput, calls=%fused_computation.19 | convolution fusion | flops 2416705536 | bytes 9437184 | tf_op jit(solution)/shard_map/rlf,lkf->lrk/dot_general | solution.py:96
  232.5 1.5 copy.66
  234.0 7.7 %all-to-all-done.2 = bf16[2,32,24,512]{3,2,0,1:T(8,128)(2,1)} async-done(((bf16[2,32,24,512]{3,2,0,1:T(8,128)(2,1)}), bf16[2,32,24,512]{3,2,0,1:T(8,128)(2,1)}, u32[]{:S(2)}, u32[]{:S(2)}) %all-to-all-start.2) | async-done | bytes 1572896 | tf_op jit(solution)/shard_map/all_to_all | solution.py:81
  241.7 6.6 %all-to-all-start.3 = ((bf16[2,32,24,512]{3,2,0,1:T(8,128)(2,1)}), bf16[2,32,24,512]{3,2,0,1:T(8,128)(2,1)}, u32[]{:S(2)}, u32[]{:S(2)}) async-start(bf16[2,32,24,512]{3,2,0,1:T(8,128)(2,1)} %copy.66), calls=%async_computation.5 | async-start | bytes 3145728 | tf_op jit(solution)/shard_map/all_to_all | solution.py:105
  248.3 4.7 %convolution_convert_fusion.2 = bf16[2,768,512]{2,1,0:T(8,128)(2,1)} fusion(bf16[768,2,768]{2,0,1:T(8,128)(2,1)} %all-gather.3.cloned.1.call-done, bf16[2,768,512]{2,1,0:T(8,128)(2,1)} %bitcast.43), kind=kOutput, calls=%fused_computation.17 | convolution fusion | flops 1208745984 | bytes 5505024 | tf_op jit(solution)/shard_map/rlf,lrk->lfk/dot_general | solution.py:102
  253.0 1.5 copy.65
  254.5 2.9 bitcast_reduce_fusion
  257.4 0.3 fusion.5
  257.7 0.1 reshape.124
  257.8 25.1 %psum.7 = f32[128,8]{1,0:T(8,128)S(1)} all-reduce(f32[128,8]{1,0:T(8,128)S(1)} %reshape.124), channel_id=1, replica_groups=mesh['dp'=8,'expert'=32] {'dp'}, use_global_device_ids=true, to_apply=%region_7.8 | all-reduce | flops 1024 | bytes 8192 | tf_op jit(solution)/shard_map/psum | solution.py:95
  282.9 0.7 copy.70
  283.6 7.1 %convolution_convert_fusion = bf16[2,512,1536]{2,1,0:T(8,128)(2,1)} fusion(bf16[2,768,512]{2,1,0:T(8,128)(2,1)} %bitcast.41, bf16[768,2,1536]{2,0,1:T(8,128)(2,1)} %all-gather.5.cloned.1.call-done), kind=kOutput, calls=%fused_computation.8 | convolution fusion | flops 2417491968 | bytes 9437184 | tf_op jit(solution)/shard_map/lrk,rlf->lkf/dot_general | solution.py:99
  290.7 0.0 all-to-all-done.3
  290.7 1.5 copy.67
  292.2 1.0 convolution_convert_fusion.5
  (4 shorter events, 0.0 us)
Async XLA Ops:
  7.2 57.9 %copy-start = (bf16[2,512,1536]{2,1,0:T(8,128)(2,1)S(1)}, bf16[2,512,1536]{2,1,0:T(8,128)(2,1)}, u32[]{:S(2)}) copy-start(bf16[2,512,1536]{2,1,0:T(8,128)(2,1)} %param.9) | copy-start | bytes 9437188
  7.2 5.0 %copy-start.4 = (bf16[128,512]{1,0:T(8,128)(2,1)S(1)}, bf16[128,512]{1,0:T(8,128)(2,1)}, u32[]{:S(2)}) copy-start(bf16[128,512]{1,0:T(8,128)(2,1)} %param.6) | copy-start | bytes 393220
  7.2 109.9 %reduce-scatter.3.cloned.1.call-start = ((), (), s32[]{:S(2)}) async-start(), calls=%async_computation.6 | async-start | bytes 5308416 | tf_op jit(solution)/shard_map/reduce_scatter | solution.py:48
  63.9 1.2 copy-start.2
  69.3 0.7 copy-start.5
  69.3 1.7 copy-start.3
  69.3 89.6 %reduce-scatter.5.cloned.1.call-start = ((), (), s32[]{:S(2)}) async-start(), calls=%async_computation.8 | async-start | bytes 2654208 | tf_op jit(solution)/shard_map/reduce_scatter | solution.py:70
  118.3 1.0 copy-start.1
  124.9 62.9 %all-gather.3.cloned.1.call-start = ((), (), s32[]{:S(2)}) async-start(), calls=%async_computation.7 | async-start | bytes 2654208 | tf_op jit(solution)/shard_map/all_gather | solution.py:66
  125.7 101.9 %all-gather.5.cloned.1.call-start = ((), (), s32[]{:S(2)}) async-start(), calls=%async_computation.9 | async-start | bytes 5308416 | tf_op jit(solution)/shard_map/all_gather | solution.py:79
  192.7 49.0 %all-to-all-start.2 = ((bf16[2,32,24,512]{3,2,0,1:T(8,128)(2,1)}), bf16[2,32,24,512]{3,2,0,1:T(8,128)(2,1)}, u32[]{:S(2)}, u32[]{:S(2)}) async-start(bf16[2,32,24,512]{3,2,0,1:T(8,128)(2,1)} %copy.64), calls=%async_computation.3 | async-start | bytes 3145728 | tf_op jit(solution)/shard_map/all_to_all | solution.py:81
  241.7 49.0 %all-to-all-start.3 = ((bf16[2,32,24,512]{3,2,0,1:T(8,128)(2,1)}), bf16[2,32,24,512]{3,2,0,1:T(8,128)(2,1)}, u32[]{:S(2)}, u32[]{:S(2)}) async-start(bf16[2,32,24,512]{3,2,0,1:T(8,128)(2,1)} %copy.66), calls=%async_computation.5 | async-start | bytes 3145728 | tf_op jit(solution)/shard_map/all_to_all | solution.py:105
Sparse Core Ops, SparseCore 0:
  69.4 39.0 reduce-scatter.2
  125.0 33.8 reduce-scatter.4
  160.8 27.0 all-gather.2
  190.1 37.3 all-gather.4

commit v2 on v1

--- a/solution.py
+++ b/solution.py
@@ -94,7 +94,10 @@
     partial_dot = jnp.sum(grad_routes * y_routes, axis=1).reshape(tok_count, top_count)
     route_grad = lax.psum(partial_dot, "dp")
     x_grad_slice = jnp.einsum(
-        "rlf,lkf->lrk", preact_grad_all, gate_up_weight, preferred_element_type=jnp.float32
+        "gclf,lkf->glck",
+        preact_grad_all.reshape(group_count, capacity, local_count, 2 * hidden_units),
+        gate_up_weight,
+        preferred_element_type=jnp.float32,
     ).astype(jnp.bfloat16)
     gate_up_grad = jnp.einsum(
         "lrk,rlf->lkf", arrived, preact_grad_all, preferred_element_type=jnp.float32
@@ -102,11 +105,14 @@
     down_grad = jnp.einsum(
         "rlf,lrk->lfk", hidden_all, grad_arrived, preferred_element_type=jnp.float32
     ).astype(jnp.bfloat16)
-    grad_back = lax.all_to_all(
-        x_grad_slice.reshape(block_shape), "expert", split_axis=1, concat_axis=1, tiled=True
+    grad_back = lax.all_to_all(x_grad_slice, "expert", split_axis=0, concat_axis=0, tiled=True)
+    token_hit_back = (
+        token_hit.reshape(tok_count, local_count, group_count, capacity)
+        .transpose(0, 2, 1, 3)
+        .reshape(tok_count, slot_count)
     )
     token_grad = jnp.dot(
-        token_hit, grad_back.reshape(slot_count, piece_width), preferred_element_type=jnp.float32
+        token_hit_back, grad_back.reshape(slot_count, piece_width), preferred_element_type=jnp.float32
     ).astype(jnp.bfloat16)
     return (layer_out, token_grad, route_grad, gate_up_grad, down_grad)
 

time: 301 us -> 302 us (level)
  transfers between devices with their start and end apart: 6 -> 6, of which waited for: 4 -> 4; matrix products, arithmetic and copies ran while one was open for 11% -> 12% of each run, Pallas kernels for 0% -> 0%
where the time goes in v2:
time: 302 us; the launch traced here: 301 us
  blocking collectives  120 us (40%)
  waiting for transfers between devices  92 us (30%)
  matrix products  36.5 us (12%)
  starting transfers between devices  16.9 us (6%)
  between operations  14 us (5%)
  local copies, waits for them, and re-layouts  12.7 us (4%)
  other arithmetic  8.92 us (3%)
    all_to_all x1, blocking collectives, layer(): lax.all_to_all(outbound.reshape(block_shape), 'expert', split_axis=1, con...  50.7 us
    all_to_all x1, blocking collectives, layer(): lax.all_to_all(grad_outbound.reshape(block_shape), 'expert', split_axis=1...  43.9 us
    reduce_scatter x1, waiting for transfers between devices, layer(): lax.psum_scatter(hidden_grad_part, 'dp', scatter_dimension=0, tiled=True)  33.3 us
    all_gather x1, waiting for transfers between devices, layer(): hidden_all = lax.all_gather(hidden_mine, 'dp', axis=0, tiled=True)  26.3 us
    psum x1, blocking collectives, layer(): route_grad = lax.psum(partial_dot, 'dp')  25.5 us
    all_gather x1, waiting for transfers between devices, layer(): preact_grad_all = lax.all_gather(preact_grad, 'dp', axis=0, tiled=True)  24.6 us
    all_to_all x1, starting transfers between devices, layer(): lax.all_to_all(out_slice.reshape(block_shape), 'expert', split_axis=1, co...  10.2 us
    dot_general x1, matrix products, layer(): jnp.einsum('lrk,rlf->lkf', arrived, preact_grad_all, preferred_element_ty...  7.16 us
  transfers between devices with their start and end apart: 6, of which 4 were waited for; matrix products, arithmetic and copies ran while one was open for 12% of the time, Pallas kernels for 0%

profile of v2, /device:TPU:2, one launch (start us, length us, event | category | flops | bytes accessed | tf_op | source)
XLA Modules:
  0.0 301.1 jit_solution(4395253339161292423)
XLA Ops:
  7.2 0.0 copy-start
  7.2 0.0 copy-start.5
  7.2 0.0 reduce-scatter.3.cloned.1.call-start
  7.2 0.9 copy.59
  8.2 0.1 reshape.116
  8.3 0.6 fusion.21
  8.9 0.1 convert_element_type.79
  9.0 0.1 fusion.32
  9.1 3.2 %fusion.1 = pred[128,1536]{1,0:T(8,128)(4,1)S(1)} fusion(s32[128,8]{1,0:T(8,128)S(1)} %fusion.32), kind=kLoop, calls=%fused_computation.4 | loop fusion | flops 2949120 | bytes 200704 | tf_op jit(solution)/shard_map/reduce_or | solution.py:31
  12.2 0.0 copy-done.5
  12.2 0.6 convolution_convert_fusion.1
  12.8 0.2 copy.64
  13.1 50.7 %all_to_all.20 = bf16[2,32,24,512]{3,2,0,1:T(8,128)(2,1)S(1)} all-to-all(bf16[2,32,24,512]{3,2,0,1:T(8,128)(2,1)S(1)} %copy.64), channel_id=1, replica_groups=mesh['dp'=8,'expert'=32] {'expert'}, dimensions={1} | all-to-all | bytes 3145728 | tf_op jit(solution)/shard_map/all_to_all | solution.py:45
  63.8 0.1 copy.65
  63.9 0.0 copy-start.2
  63.9 1.2 copy-done.2
  65.1 0.0 copy-done
  65.1 4.2 %convert_bitcast_fusion = bf16[768,2,1536]{2,0,1:T(8,128)(2,1)} fusion(bf16[2,768,512]{2,1,0:T(8,128)(2,1)S(1)} %bitcast.55, bf16[2,512,1536]{2,1,0:T(8,128)(2,1)S(1)} %copy-done), kind=kOutput, calls=%fused_computation.7 | convolution fusion | flops 2418278400 | bytes 9437184 | tf_op jit(solution)/shard_map/lrk,lkf->rlf/dot_general | solution.py:49
  69.3 0.0 copy-start.6
  69.3 0.0 reduce-scatter.3.cloned.1.call-update
  69.3 0.0 reduce-scatter.5.cloned.1.call-start
  69.4 0.6 copy-done.6
  70.0 0.1 copy.58
  70.1 0.1 mul.75
  70.2 0.8 select_reduce_fusion
  71.0 0.0 copy-done.3
  71.0 0.6 fusion.7
  71.7 0.2 copy.66
  71.9 43.9 %all_to_all.21 = bf16[2,32,24,512]{3,2,0,1:T(8,128)(2,1)S(1)} all-to-all(bf16[2,32,24,512]{3,2,0,1:T(8,128)(2,1)S(1)} %copy.66), channel_id=1, replica_groups=mesh['dp'=8,'expert'=32] {'expert'}, dimensions={1} | all-to-all | bytes 3145728 | tf_op jit(solution)/shard_map/all_to_all | solution.py:56
  115.8 1.3 copy.67
  117.1 1.2 convert_element_type.83
  118.3 0.0 copy-start.1
  118.3 1.0 copy-done.1
  119.3 0.9 multiply_convert_fusion
  120.2 4.7 %convert_bitcast_fusion.1 = bf16[768,2,768]{2,0,1:T(8,128)(2,1)} fusion(bf16[2,768,512]{2,1,0:T(8,128)(2,1)} %bitcast.57, bf16[2,768,512]{2,1,0:T(8,128)(2,1)} %param.10), kind=kOutput, calls=%fused_computation.16 | convolution fusion | flops 1209139200 | bytes 5505024 | tf_op jit(solution)/shard_map/lrk,lfk->rlf/dot_general | solution.py:67
  124.9 0.0 reduce-scatter.5.cloned.1.call-update
  124.9 0.0 all-gather.3.cloned.1.call-start
  125.0 0.7 all-gather.3.cloned.1.call-update
  125.7 0.0 all-gather.5.cloned.1.call-start
  125.7 33.3 %reduce-scatter.5.cloned.1.call-done = bf16[96,2,768]{2,0,1:T(8,128)(2,1)} async-done(((bf16[768,2,768]{2,0,1:T(8,128)(2,1)}), bf16[96,2,768]{2,0,1:T(8,128)(2,1)}) %reduce-scatter.5.cloned.1.call-update) | async-done | bytes 294928 | tf_op jit(solution)/shard_map/reduce_scatter | solution.py:70
  159.0 1.6 fusion.25
  160.7 0.9 pad_maximum_fusion
  161.5 0.0 all-gather.5.cloned.1.call-update
  161.5 26.3 %all-gather.3.cloned.1.call-done = bf16[768,2,768]{2,0,1:T(8,128)(2,1)} async-done(((bf16[96,2,768]{2,0,1:T(8,128)(2,1)}), bf16[768,2,768]{2,0,1:T(8,128)(2,1)}) %all-gather.3.cloned.1.call-update) | async-done | bytes 2359312 | tf_op jit(solution)/shard_map/all_gather | solution.py:66
  187.8 3.5 %convolution_convert_fusion.3 = bf16[2,768,512]{2,1,0:T(8,128)(2,1)S(1)} fusion(bf16[768,2,768]{2,0,1:T(8,128)(2,1)} %all-gather.3.cloned.1.call-done, bf16[2,768,512]{2,1,0:T(8,128)(2,1)} %param.10), kind=kOutput, calls=%fused_computation.21 | convolution fusion | flops 1208745984 | bytes 5505024 | tf_op jit(solution)/shard_map/rlf,lfk->lrk/dot_general | solution.py:72
  191.3 1.4 copy.68
  192.7 10.2 %all-to-all-start.2 = ((bf16[2,32,24,512]{3,2,0,1:T(8,128)(2,1)}), bf16[2,32,24,512]{3,2,0,1:T(8,128)(2,1)}, u32[]{:S(2)}, u32[]{:S(2)}) async-start(bf16[2,32,24,512]{3,2,0,1:T(8,128)(2,1)} %copy.68), calls=%async_computation.3 | async-start | bytes 3145728 | tf_op jit(solution)/shard_map/all_to_all | solution.py:81
  202.9 24.6 %all-gather.5.cloned.1.call-done = bf16[768,2,1536]{2,0,1:T(8,128)(2,1)} async-done(((bf16[96,2,1536]{2,0,1:T(8,128)(2,1)}), bf16[768,2,1536]{2,0,1:T(8,128)(2,1)}) %all-gather.5.cloned.1.call-update) | async-done | bytes 4718608 | tf_op jit(solution)/shard_map/all_gather | solution.py:79
  227.5 5.0 %fusion.14 = bf16[32,2,24,512]{3,0,2,1:T(8,128)(2,1)S(1)} fusion(bf16[2,512,1536]{2,1,0:T(8,128)(2,1)S(1)} %copy-done, bf16[32,24,2,1536]{3,1,0,2:T(8,128)(2,1)} %bitcast.62), kind=kOutput, calls=%fused_computation.23 | convolution fusion | flops 2416705536 | bytes 9437184 | tf_op jit(solution)/shard_map/gclf,lkf->glck/dot_general | solution.py:96
  232.5 2.1 copy.72
  234.6 7.1 %all-to-all-done.2 = bf16[2,32,24,512]{3,2,0,1:T(8,128)(2,1)} async-done(((bf16[2,32,24,512]{3,2,0,1:T(8,128)(2,1)}), bf16[2,32,24,512]{3,2,0,1:T(8,128)(2,1)}, u32[]{:S(2)}, u32[]{:S(2)}) %all-to-all-start.2) | async-done | bytes 1572896 | tf_op jit(solution)/shard_map/all_to_all | solution.py:81
  241.7 6.6 %all-to-all-start.3 = ((bf16[32,2,24,512]{3,2,1,0:T(8,128)(2,1)}), bf16[32,2,24,512]{3,2,1,0:T(8,128)(2,1)}, u32[]{:S(2)}, u32[]{:S(2)}) async-start(bf16[32,2,24,512]{3,2,1,0:T(8,128)(2,1)} %copy.72), calls=%async_computation.5 | async-start | bytes 3145728 | tf_op jit(solution)/shard_map/all_to_all | solution.py:108
  248.2 1.0 copy.70
  249.2 4.7 %convolution_convert_fusion.2 = bf16[2,768,512]{2,1,0:T(8,128)(2,1)} fusion(bf16[768,2,768]{2,0,1:T(8,128)(2,1)} %all-gather.3.cloned.1.call-done, bf16[2,768,512]{2,1,0:T(8,128)(2,1)} %bitcast.58), kind=kOutput, calls=%fused_computation.20 | convolution fusion | flops 1208745984 | bytes 5505024 | tf_op jit(solution)/shard_map/rlf,lrk->lfk/dot_general | solution.py:105
  253.9 1.5 copy.69
  255.4 2.9 bitcast_reduce_fusion
  258.3 0.3 fusion.8
  258.6 0.1 reshape.126
  258.7 25.5 %psum.7 = f32[128,8]{1,0:T(8,128)S(1)} all-reduce(f32[128,8]{1,0:T(8,128)S(1)} %reshape.126), channel_id=1, replica_groups=mesh['dp'=8,'expert'=32] {'dp'}, use_global_device_ids=true, to_apply=%region_7.8 | all-reduce | flops 1024 | bytes 8192 | tf_op jit(solution)/shard_map/psum | solution.py:95
  284.2 0.7 copy.76
  284.9 7.2 %convolution_convert_fusion = bf16[2,512,1536]{2,1,0:T(8,128)(2,1)} fusion(bf16[2,768,512]{2,1,0:T(8,128)(2,1)} %bitcast.56, bf16[768,2,1536]{2,0,1:T(8,128)(2,1)} %all-gather.5.cloned.1.call-done), kind=kOutput, calls=%fused_computation.10 | convolution fusion | flops 2417491968 | bytes 9437184 | tf_op jit(solution)/shard_map/lrk,rlf->lkf/dot_general | solution.py:102
  292.0 0.0 all-to-all-done.3
  292.1 0.0 copy-done.4
  292.1 2.5 fusion.20
  (6 shorter events, 0.0 us)
Async XLA Ops:
  7.2 57.9 %copy-start = (bf16[2,512,1536]{2,1,0:T(8,128)(2,1)S(1)}, bf16[2,512,1536]{2,1,0:T(8,128)(2,1)}, u32[]{:S(2)}) copy-start(bf16[2,512,1536]{2,1,0:T(8,128)(2,1)} %param.9) | copy-start | bytes 9437188
  7.2 5.0 %copy-start.5 = (bf16[128,512]{1,0:T(8,128)(2,1)S(1)}, bf16[128,512]{1,0:T(8,128)(2,1)}, u32[]{:S(2)}) copy-start(bf16[128,512]{1,0:T(8,128)(2,1)} %param.6) | copy-start | bytes 393220
  7.2 109.9 %reduce-scatter.3.cloned.1.call-start = ((), (), s32[]{:S(2)}) async-start(), calls=%async_computation.6 | async-start | bytes 5308416 | tf_op jit(solution)/shard_map/reduce_scatter | solution.py:48
  63.9 1.2 copy-start.2
  69.3 0.7 copy-start.6
  69.3 1.7 copy-start.3
  69.3 89.7 %reduce-scatter.5.cloned.1.call-start = ((), (), s32[]{:S(2)}) async-start(), calls=%async_computation.8 | async-start | bytes 2654208 | tf_op jit(solution)/shard_map/reduce_scatter | solution.py:70
  118.3 1.0 copy-start.1
  124.9 62.9 %all-gather.3.cloned.1.call-start = ((), (), s32[]{:S(2)}) async-start(), calls=%async_computation.7 | async-start | bytes 2654208 | tf_op jit(solution)/shard_map/all_gather | solution.py:66
  125.7 101.8 %all-gather.5.cloned.1.call-start = ((), (), s32[]{:S(2)}) async-start(), calls=%async_computation.9 | async-start | bytes 5308416 | tf_op jit(solution)/shard_map/all_gather | solution.py:79
  192.7 49.0 %all-to-all-start.2 = ((bf16[2,32,24,512]{3,2,0,1:T(8,128)(2,1)}), bf16[2,32,24,512]{3,2,0,1:T(8,128)(2,1)}, u32[]{:S(2)}, u32[]{:S(2)}) async-start(bf16[2,32,24,512]{3,2,0,1:T(8,128)(2,1)} %copy.68), calls=%async_computation.3 | async-start | bytes 3145728 | tf_op jit(solution)/shard_map/all_to_all | solution.py:81
  241.7 50.4 %all-to-all-start.3 = ((bf16[32,2,24,512]{3,2,1,0:T(8,128)(2,1)}), bf16[32,2,24,512]{3,2,1,0:T(8,128)(2,1)}, u32[]{:S(2)}, u32[]{:S(2)}) async-start(bf16[32,2,24,512]{3,2,1,0:T(8,128)(2,1)} %copy.72), calls=%async_computation.5 | async-start | bytes 3145728 | tf_op jit(solution)/shard_map/all_to_all | solution.py:108
  284.9 7.2 %copy-start.4 = (pred[128,1536]{0,1:T(8,128)(4,1)S(1)}, pred[128,1536]{0,1:T(8,128)(4,1)}, u32[]{:S(2)}) copy-start(pred[128,1536]{0,1:T(8,128)(4,1)} %copy.70) | copy-start | bytes 589828
Sparse Core Ops, SparseCore 0:
  69.4 39.0 reduce-scatter.2
  125.0 33.9 reduce-scatter.4
  160.8 26.8 all-gather.2
  190.1 37.3 all-gather.4

commit v3 on v1

--- a/solution.py
+++ b/solution.py
@@ -33,13 +33,20 @@
     )
     weight_flat = route_weights.reshape(-1)
     slot_weight = jnp.sum(jnp.where(route_hit, weight_flat[:, None], 0.0), axis=0)
+    route_pick = route_hit.astype(jnp.bfloat16)
     outbound = lax.dot_general(
-        token_hit, tokens, (((0,), (0,)), ((), ())), preferred_element_type=jnp.float32
+        route_pick,
+        jnp.repeat(tokens, top_count, axis=0),
+        (((0,), (0,)), ((), ())),
+        preferred_element_type=jnp.float32,
     ).astype(jnp.bfloat16)
     grad_outbound = (
         slot_weight[:, None]
         * lax.dot_general(
-            token_hit, out_grad, (((0,), (0,)), ((), ())), preferred_element_type=jnp.float32
+            route_pick,
+            jnp.repeat(out_grad, top_count, axis=0),
+            (((0,), (0,)), ((), ())),
+            preferred_element_type=jnp.float32,
         )
     ).astype(jnp.bfloat16)
     arrived = lax.all_to_all(

time: 301 us -> 304 us (level)
  matrix products: 34.9 us -> 38.2 us
    dot_general x2, matrix products: 1.25 us -> 4.44 us  [the longest x1 2.27 us: layer(): lax.dot_general(route_pick, jnp.repeat(out_grad, top_count, axis=0), (((0...]
  transfers between devices with their start and end apart: 6 -> 6, of which waited for: 4 -> 4; matrix products, arithmetic and copies ran while one was open for 11% -> 13% of each run, Pallas kernels for 0% -> 0%
where the time goes in v3:
time: 304 us; the launch traced here: 303 us
  blocking collectives  120 us (39%)
  waiting for transfers between devices  92.6 us (30%)
  matrix products  38.2 us (13%)
  starting transfers between devices  16.9 us (6%)
  between operations  14 us (5%)
  local copies, waits for them, and re-layouts  12.6 us (4%)
  other arithmetic  8.95 us (3%)
    all_to_all x1, blocking collectives, layer(): lax.all_to_all(outbound.reshape(block_shape), 'expert', split_axis=1, con...  50.7 us
    all_to_all x1, blocking collectives, layer(): lax.all_to_all(grad_outbound.reshape(block_shape), 'expert', split_axis=1...  43.9 us
    reduce_scatter x1, waiting for transfers between devices, layer(): lax.psum_scatter(hidden_grad_part, 'dp', scatter_dimension=0, tiled=True)  33.2 us
    all_gather x1, waiting for transfers between devices, layer(): hidden_all = lax.all_gather(hidden_mine, 'dp', axis=0, tiled=True)  26.3 us
    psum x1, blocking collectives, layer(): route_grad = lax.psum(partial_dot, 'dp')  25.4 us
    all_gather x1, waiting for transfers between devices, layer(): preact_grad_all = lax.all_gather(preact_grad, 'dp', axis=0, tiled=True)  24.6 us
    all_to_all x1, starting transfers between devices, layer(): lax.all_to_all(out_slice.reshape(block_shape), 'expert', split_axis=1, co...  10.2 us
    all_to_all x1, waiting for transfers between devices, layer(): lax.all_to_all(out_slice.reshape(block_shape), 'expert', split_axis=1, co...  7.75 us
  transfers between devices with their start and end apart: 6, of which 4 were waited for; matrix products, arithmetic and copies ran while one was open for 13% of the time, Pallas kernels for 0%

profile of v3, /device:TPU:2, one launch (start us, length us, event | category | flops | bytes accessed | tf_op | source)
XLA Modules:
  0.0 303.2 jit_solution(7688738280412796629)
XLA Ops:
  7.2 0.0 copy-start
  7.2 0.0 copy-start.5
  7.2 0.0 reduce-scatter.3.cloned.1.call-start
  7.2 0.9 copy.55
  8.2 0.1 reshape.119
  8.3 0.6 fusion.13
  8.9 0.0 copy-done.5
  8.9 2.2 fusion.10
  11.1 0.2 copy.56
  11.3 50.7 %all_to_all.20 = bf16[2,32,24,512]{3,2,0,1:T(8,128)(2,1)S(1)} all-to-all(bf16[2,32,24,512]{3,2,0,1:T(8,128)(2,1)S(1)} %copy.56), channel_id=1, replica_groups=mesh['dp'=8,'expert'=32] {'expert'}, dimensions={1} | all-to-all | bytes 3145728 | tf_op jit(solution)/shard_map/all_to_all | solution.py:52
  62.0 0.1 copy.57
  62.1 0.0 copy-start.2
  62.2 1.2 copy-done.2
  63.3 0.0 copy-done
  63.3 4.2 %convert_bitcast_fusion = bf16[768,2,1536]{2,0,1:T(8,128)(2,1)} fusion(bf16[2,768,512]{2,1,0:T(8,128)(2,1)S(1)} %bitcast.37, bf16[2,512,1536]{2,1,0:T(8,128)(2,1)S(1)} %copy-done), kind=kOutput, calls=%fused_computation.7 | convolution fusion | flops 2418278400 | bytes 9437184 | tf_op jit(solution)/shard_map/lrk,lkf->rlf/dot_general | solution.py:56
  67.5 0.0 copy-start.4
  67.5 0.0 copy-start.3
  67.5 0.0 reduce-scatter.3.cloned.1.call-update
  67.6 0.0 reduce-scatter.5.cloned.1.call-start
  67.6 0.6 copy-done.4
  68.2 0.1 copy.54
  68.3 0.1 mul.75
  68.4 0.8 select_reduce_fusion
  69.3 0.0 copy-done.3
  69.3 2.3 fusion.9
  71.5 0.2 copy.58
  71.8 43.9 %all_to_all.21 = bf16[2,32,24,512]{3,2,0,1:T(8,128)(2,1)S(1)} all-to-all(bf16[2,32,24,512]{3,2,0,1:T(8,128)(2,1)S(1)} %copy.58), channel_id=1, replica_groups=mesh['dp'=8,'expert'=32] {'expert'}, dimensions={1} | all-to-all | bytes 3145728 | tf_op jit(solution)/shard_map/all_to_all | solution.py:63
  115.7 1.3 copy.59
  117.0 1.2 convert_element_type.76
  118.2 0.0 copy-start.1
  118.2 1.0 copy-done.1
  119.2 0.9 multiply_convert_fusion
  120.1 4.7 %convert_bitcast_fusion.1 = bf16[768,2,768]{2,0,1:T(8,128)(2,1)} fusion(bf16[2,768,512]{2,1,0:T(8,128)(2,1)} %bitcast.39, bf16[2,768,512]{2,1,0:T(8,128)(2,1)} %param.10), kind=kOutput, calls=%fused_computation.17 | convolution fusion | flops 1209139200 | bytes 5505024 | tf_op jit(solution)/shard_map/lrk,lfk->rlf/dot_general | solution.py:74
  124.8 0.0 reduce-scatter.5.cloned.1.call-update
  124.8 0.0 all-gather.3.cloned.1.call-start
  124.8 0.7 all-gather.3.cloned.1.call-update
  125.5 0.0 all-gather.5.cloned.1.call-start
  125.6 33.2 %reduce-scatter.5.cloned.1.call-done = bf16[96,2,768]{2,0,1:T(8,128)(2,1)} async-done(((bf16[768,2,768]{2,0,1:T(8,128)(2,1)}), bf16[96,2,768]{2,0,1:T(8,128)(2,1)}) %reduce-scatter.5.cloned.1.call-update) | async-done | bytes 294928 | tf_op jit(solution)/shard_map/reduce_scatter | solution.py:77
  158.8 1.6 fusion.17
  160.4 0.9 pad_maximum_fusion
  161.3 0.0 all-gather.5.cloned.1.call-update
  161.3 26.3 %all-gather.3.cloned.1.call-done = bf16[768,2,768]{2,0,1:T(8,128)(2,1)} async-done(((bf16[96,2,768]{2,0,1:T(8,128)(2,1)}), bf16[768,2,768]{2,0,1:T(8,128)(2,1)}) %all-gather.3.cloned.1.call-update) | async-done | bytes 2359312 | tf_op jit(solution)/shard_map/all_gather | solution.py:73
  187.7 3.5 %convolution_convert_fusion.2 = bf16[2,768,512]{2,1,0:T(8,128)(2,1)S(1)} fusion(bf16[768,2,768]{2,0,1:T(8,128)(2,1)} %all-gather.3.cloned.1.call-done, bf16[2,768,512]{2,1,0:T(8,128)(2,1)} %param.10), kind=kOutput, calls=%fused_computation.21 | convolution fusion | flops 1208745984 | bytes 5505024 | tf_op jit(solution)/shard_map/rlf,lfk->lrk/dot_general | solution.py:79
  191.2 1.4 copy.60
  192.5 10.2 %all-to-all-start.2 = ((bf16[2,32,24,512]{3,2,0,1:T(8,128)(2,1)}), bf16[2,32,24,512]{3,2,0,1:T(8,128)(2,1)}, u32[]{:S(2)}, u32[]{:S(2)}) async-start(bf16[2,32,24,512]{3,2,0,1:T(8,128)(2,1)} %copy.60), calls=%async_computation.3 | async-start | bytes 3145728 | tf_op jit(solution)/shard_map/all_to_all | solution.py:88
  202.7 24.6 %all-gather.5.cloned.1.call-done = bf16[768,2,1536]{2,0,1:T(8,128)(2,1)} async-done(((bf16[96,2,1536]{2,0,1:T(8,128)(2,1)}), bf16[768,2,1536]{2,0,1:T(8,128)(2,1)}) %all-gather.5.cloned.1.call-update) | async-done | bytes 4718608 | tf_op jit(solution)/shard_map/all_gather | solution.py:86
  227.3 5.0 %convolution_convert_fusion.3 = bf16[2,768,512]{2,1,0:T(8,128)(2,1)S(1)} fusion(bf16[768,2,1536]{2,0,1:T(8,128)(2,1)} %all-gather.5.cloned.1.call-done, bf16[2,512,1536]{2,1,0:T(8,128)(2,1)S(1)} %copy-done), kind=kOutput, calls=%fused_computation.22 | convolution fusion | flops 2416705536 | bytes 9437184 | tf_op jit(solution)/shard_map/rlf,lkf->lrk/dot_general | solution.py:103
  232.3 1.5 copy.66
  233.8 7.7 %all-to-all-done.2 = bf16[2,32,24,512]{3,2,0,1:T(8,128)(2,1)} async-done(((bf16[2,32,24,512]{3,2,0,1:T(8,128)(2,1)}), bf16[2,32,24,512]{3,2,0,1:T(8,128)(2,1)}, u32[]{:S(2)}, u32[]{:S(2)}) %all-to-all-start.2) | async-done | bytes 1572896 | tf_op jit(solution)/shard_map/all_to_all | solution.py:88
  241.5 6.6 %all-to-all-start.3 = ((bf16[2,32,24,512]{3,2,0,1:T(8,128)(2,1)}), bf16[2,32,24,512]{3,2,0,1:T(8,128)(2,1)}, u32[]{:S(2)}, u32[]{:S(2)}) async-start(bf16[2,32,24,512]{3,2,0,1:T(8,128)(2,1)} %copy.66), calls=%async_computation.5 | async-start | bytes 3145728 | tf_op jit(solution)/shard_map/all_to_all | solution.py:112
  248.1 0.1 convert_element_type.83
  248.2 0.1 fusion.26
  248.3 3.2 %fusion.3 = pred[128,1536]{1,0:T(8,128)(4,1)S(1)} fusion(s32[128,8]{1,0:T(8,128)S(1)} %fusion.26), kind=kLoop, calls=%fused_computation.6 | loop fusion | flops 2949120 | bytes 200704 | tf_op jit(solution)/shard_map/reduce_or | solution.py:31
  251.4 4.7 %convolution_convert_fusion.1 = bf16[2,768,512]{2,1,0:T(8,128)(2,1)} fusion(bf16[768,2,768]{2,0,1:T(8,128)(2,1)} %all-gather.3.cloned.1.call-done, bf16[2,768,512]{2,1,0:T(8,128)(2,1)} %bitcast.40), kind=kOutput, calls=%fused_computation.20 | convolution fusion | flops 1208745984 | bytes 5505024 | tf_op jit(solution)/shard_map/rlf,lrk->lfk/dot_general | solution.py:109
  256.1 1.5 copy.61
  257.6 2.9 bitcast_reduce_fusion
  260.5 0.3 multiply_reduce_fusion
  260.9 0.1 reshape.131
  260.9 25.4 %psum.7 = f32[128,8]{1,0:T(8,128)S(1)} all-reduce(f32[128,8]{1,0:T(8,128)S(1)} %reshape.131), channel_id=1, replica_groups=mesh['dp'=8,'expert'=32] {'dp'}, use_global_device_ids=true, to_apply=%region_7.8 | all-reduce | flops 1024 | bytes 8192 | tf_op jit(solution)/shard_map/psum | solution.py:102
  286.3 0.7 copy.70
  287.0 7.1 %convolution_convert_fusion = bf16[2,512,1536]{2,1,0:T(8,128)(2,1)} fusion(bf16[2,768,512]{2,1,0:T(8,128)(2,1)} %bitcast.38, bf16[768,2,1536]{2,0,1:T(8,128)(2,1)} %all-gather.5.cloned.1.call-done), kind=kOutput, calls=%fused_computation.10 | convolution fusion | flops 2417491968 | bytes 9437184 | tf_op jit(solution)/shard_map/lrk,rlf->lkf/dot_general | solution.py:106
  294.1 0.0 all-to-all-done.3
  294.1 1.5 copy.67
  295.6 1.0 convolution_convert_fusion.4
  (3 shorter events, 0.0 us)
Async XLA Ops:
  7.2 56.2 %copy-start = (bf16[2,512,1536]{2,1,0:T(8,128)(2,1)S(1)}, bf16[2,512,1536]{2,1,0:T(8,128)(2,1)}, u32[]{:S(2)}) copy-start(bf16[2,512,1536]{2,1,0:T(8,128)(2,1)} %param.9) | copy-start | bytes 9437188
  7.2 1.7 copy-start.5
  7.2 109.8 %reduce-scatter.3.cloned.1.call-start = ((), (), s32[]{:S(2)}) async-start(), calls=%async_computation.6 | async-start | bytes 5308416 | tf_op jit(solution)/shard_map/reduce_scatter | solution.py:55
  62.1 1.2 copy-start.2
  67.5 0.7 copy-start.4
  67.5 1.7 copy-start.3
  67.6 91.2 %reduce-scatter.5.cloned.1.call-start = ((), (), s32[]{:S(2)}) async-start(), calls=%async_computation.8 | async-start | bytes 2654208 | tf_op jit(solution)/shard_map/reduce_scatter | solution.py:77
  118.2 1.0 copy-start.1
  124.8 62.9 %all-gather.3.cloned.1.call-start = ((), (), s32[]{:S(2)}) async-start(), calls=%async_computation.7 | async-start | bytes 2654208 | tf_op jit(solution)/shard_map/all_gather | solution.py:73
  125.5 101.8 %all-gather.5.cloned.1.call-start = ((), (), s32[]{:S(2)}) async-start(), calls=%async_computation.9 | async-start | bytes 5308416 | tf_op jit(solution)/shard_map/all_gather | solution.py:86
  192.5 49.0 %all-to-all-start.2 = ((bf16[2,32,24,512]{3,2,0,1:T(8,128)(2,1)}), bf16[2,32,24,512]{3,2,0,1:T(8,128)(2,1)}, u32[]{:S(2)}, u32[]{:S(2)}) async-start(bf16[2,32,24,512]{3,2,0,1:T(8,128)(2,1)} %copy.60), calls=%async_computation.3 | async-start | bytes 3145728 | tf_op jit(solution)/shard_map/all_to_all | solution.py:88
  241.5 52.6 %all-to-all-start.3 = ((bf16[2,32,24,512]{3,2,0,1:T(8,128)(2,1)}), bf16[2,32,24,512]{3,2,0,1:T(8,128)(2,1)}, u32[]{:S(2)}, u32[]{:S(2)}) async-start(bf16[2,32,24,512]{3,2,0,1:T(8,128)(2,1)} %copy.66), calls=%async_computation.5 | async-start | bytes 3145728 | tf_op jit(solution)/shard_map/all_to_all | solution.py:112
Sparse Core Ops, SparseCore 0:
  67.7 39.0 reduce-scatter.2
  124.9 33.8 reduce-scatter.4
  160.6 26.9 all-gather.2
  189.9 37.3 all-gather.4
